TPU v7x, 512 devices: a whole 4x8x8 slice. The times are simulated.
512 devices in a mesh: segment: 8 (over z), gy: 64 (over x, y, core).
Axes of the slice: x: 4, y: 8, z: 8, core: 2. Of those that a mesh axis runs over, the one named last changes fastest.
Arguments:
- acts: bfloat16 [8, 8, 128, 32, 256], P('segment', None, 'gy'), may hold values from -6 to 6
- grad_out: bfloat16 [8, 128, 32, 256], P('segment', 'gy'), may hold values from -6 to 6
- w_plane: bfloat16 [8, 3, 3, 32, 32], P('segment'), may hold values from -0.375 to 0.375
- w_depth: bfloat16 [8, 3, 32, 32], P('segment'), may hold values from -0.625 to 0.625
- tiles: int32 [64, 12], P('gy'), may hold values from -1 to 15, as said below
Outputs:
- grad_in: bfloat16 [8, 128, 32, 256], P('segment', 'gy')
- grad_plane: float32 [8, 3, 3, 32, 32], P('segment')
- grad_depth: float32 [8, 3, 32, 32], P('segment')
Inputs may be any that keep to these rules, and one draw needn't show every extreme that they name: Row s lists distinct tiles z * 2 + x-tile of slab s in its first entries and -1 after them; each row lists 1 to 12 tiles, and some row lists exactly 12.
All inputs are finite; a program needn't handle non-finite values.
Results may differ from a plain program's by a relative error of at most 0.02.
Values may be sent and summed in bfloat16 or wider, within the bound.
No kernel may reach another device: no remote copies, remote signals or barrier semaphores. Data moves between devices by JAX's collectives and lax.ppermute only.
A program may use at most 64 MiB of HBM per device.

v0:
```python
import math
import jax
import jax.numpy as jnp
from jax import lax
from jax.sharding import PartitionSpec as P

TILE = 128


def padded_2(block, sides, width):
    for axis, dim in sides:
        count = lax.axis_size(axis)
        forward = [(i, i + 1) for i in range(count - 1)]
        backward = [(target, source) for source, target in forward]
        low = lax.ppermute(
            lax.slice_in_dim(block, block.shape[dim] - width, None, axis=dim), axis, forward
        )
        high = lax.ppermute(lax.slice_in_dim(block, 0, width, axis=dim), axis, backward)
        block = jnp.concatenate([low, block, high], axis=dim)
    return block


def width_pad(field):
    return jnp.pad(field, [(0, 0)] * (field.ndim - 1) + [(1, 1)])


def plane_conv_all(rows_in, kernel, height, width):
    padded = width_pad(rows_in)
    total = None
    for i in range(3):
        for j in range(3):
            term = jnp.einsum(
                "loc,lzycx->lzyox",
                kernel[:, i, j],
                padded[:, :, i : i + height, :, j : j + width],
                preferred_element_type=jnp.float32,
            )
            total = term if total is None else total + term
    return total


def depth_conv_all(deep, kernel, depth):
    total = None
    for k in range(3):
        term = jnp.einsum(
            "loc,lzycx->lzyox",
            kernel[:, k],
            deep[:, k : k + depth],
            preferred_element_type=jnp.float32,
        )
        total = term if total is None else total + term
    return total


def plane_back(rows_grad, kernel, height, width):
    padded = width_pad(rows_grad)
    total = None
    for i in range(3):
        for j in range(3):
            term = jnp.einsum(
                "oc,...yox->...ycx",
                kernel[i, j],
                padded[..., 2 - i : 2 - i + height, :, 2 - j : 2 - j + width],
                preferred_element_type=jnp.float32,
            )
            total = term if total is None else total + term
    return total


def plane_taps(grad_mid, rows_in, height, width):
    padded = width_pad(rows_in)
    rows_out = []
    for i in range(3):
        row_taps = []
        for j in range(3):
            row_taps.append(
                jnp.einsum(
                    "...yox,...ycx->oc",
                    grad_mid,
                    padded[..., i : i + height, :, j : j + width],
                    preferred_element_type=jnp.float32,
                )
            )
        rows_out.append(jnp.stack(row_taps))
    return jnp.stack(rows_out)


def depth_back(mix_deep, kernel, depth):
    total = None
    for k in range(3):
        term = jnp.einsum(
            "oc,zyox->zycx",
            kernel[k],
            mix_deep[2 - k : 2 - k + depth],
            preferred_element_type=jnp.float32,
        )
        total = term if total is None else total + term
    return total


def depth_taps(grad_mix, deep, depth):
    return jnp.stack(
        [
            jnp.einsum(
                "zyox,zycx->oc", grad_mix, deep[k : k + depth], preferred_element_type=jnp.float32
            )
            for k in range(3)
        ]
    )


def silu_slope(value):
    sig = jax.nn.sigmoid(value)
    return sig * (1.0 + value * (1.0 - sig))


def local(acts, grad_out, w_plane, w_depth, tiles):
    sections = acts.shape[1]
    height = acts.shape[2]
    width = acts.shape[4]
    chans = w_plane.shape[3]
    count = lax.axis_size("segment")
    layers = count * acts.shape[0]
    zs = grad_out.shape[0]
    scale = 1.0 / math.sqrt(sections * height * lax.axis_size("gy") * width)
    segment = lax.axis_index("segment")
    mine = lax.all_to_all(acts, "segment", 1, 0, tiled=True)
    plane_w = lax.all_gather(w_plane, "segment", axis=0, tiled=True)
    depth_w = lax.all_gather(w_depth, "segment", axis=0, tiled=True)
    ids = (segment * zs + jnp.arange(zs, dtype=jnp.int32))[:, None] * (width // TILE) + jnp.arange(
        width // TILE, dtype=jnp.int32
    )[None, :]
    hit = jnp.any(tiles[0][None, None, :] == ids[:, :, None], axis=2)
    mask_full = jnp.repeat(hit.astype(jnp.float32), TILE, axis=1)[:, None, None, :]
    rows_own = padded_2(mine, (("gy", 2),), 1)
    mid = plane_conv_all(rows_own, plane_w, height, width).astype(jnp.bfloat16)
    deep = padded_2(mid, (("segment", 1),), 1)
    value = depth_conv_all(deep, depth_w, zs)
    factor = silu_slope(value) * mask_full[None]
    grad = grad_out
    plane_list = [None] * layers
    depth_list = [None] * layers
    for layer in reversed(range(layers)):
        grad_mix = (grad.astype(jnp.float32) * factor[layer]).astype(jnp.bfloat16)
        mix_deep = padded_2(grad_mix, (("segment", 0),), 1)
        grad_mid = depth_back(mix_deep, depth_w[layer], zs).astype(jnp.bfloat16)
        rows_grad = padded_2(grad_mid, (("gy", 1),), 1)
        grad = (
            grad.astype(jnp.float32) + plane_back(rows_grad, plane_w[layer], height, width)
        ).astype(jnp.bfloat16)
        depth_list[layer] = depth_taps(grad_mix, deep[layer], zs)
        plane_list[layer] = plane_taps(grad_mid, rows_own[layer], height, width)
    planes = jnp.stack(plane_list).reshape(layers, -1)
    depths = jnp.stack(depth_list).reshape(layers, -1)
    flat = jnp.concatenate([planes, depths], axis=1) * scale
    flat = lax.psum_scatter(flat, "segment", scatter_dimension=0, tiled=True)
    flat = lax.psum(flat, "gy")
    cut = planes.shape[1]
    plane_sum = flat[:, :cut].reshape(-1, 3, 3, chans, chans)
    depth_sum = flat[:, cut:].reshape(-1, 3, chans, chans)
    return (grad, plane_sum, depth_sum)


def solution(mesh):
    placed = (
        P("segment", None, "gy", None, None),
        P("segment", "gy", None, None),
        P("segment", None, None, None, None),
        P("segment", None, None, None),
        P("gy", None),
    )
    return jax.shard_map(
        local,
        mesh=mesh,
        in_specs=placed,
        out_specs=(
            P("segment", "gy", None, None),
            P("segment", None, None, None, None),
            P("segment", None, None, None),
        ),
        check_vma=False,
    )
```

profile of v0, /device:TPU:64, one launch (start us, length us, event | category | flops | bytes accessed | tf_op | source)
XLA Modules:
  0.0 603.1 jit_solution(2332710889217415071)
XLA Ops:
  7.2 10.0 %all-to-all-start = ((bf16[1,8,2,32,256]{4,3,2,0,1:T(8,128)(2,1)}), bf16[1,8,2,32,256]{4,3,2,0,1:T(8,128)(2,1)S(1)}, u32[]{:S(2)}, u32[]{:S(2)}) async-start(bf16[1,8,2,32,256]{4,3,2,0,1:T(8,128)(2,1)} %bitcast.2011), calls=%async_computation | async-start | bytes 524288 | tf_op jit(solution)/shard_map/all_to_all | solution.py:127
  18.7 26.2 %all_gather.7 = bf16[8,3,32,32]{3,2,0,1:T(8,128)(2,1)S(1)} all-gather(bf16[1,3,32,32]{3,2,0,1:T(8,128)(2,1)S(1)} %bitcast.2013), channel_id=1, replica_groups=mesh['segment'=8,'gy'=64] {'segment'}, dimensions={0}, use_global_device_ids=true | all-gather | bytes 55296 | tf_op jit(solution)/shard_map/all_gather | solution.py:129
  44.9 25.8 %all_gather.6 = bf16[8,3,3,32,32]{4,3,0,2,1:T(8,128)(2,1)S(1)} all-gather(bf16[1,3,3,32,32]{4,3,0,2,1:T(8,128)(2,1)S(1)} %bitcast.2012), channel_id=1, replica_groups=mesh['segment'=8,'gy'=64] {'segment'}, dimensions={0}, use_global_device_ids=true | all-gather | bytes 165888 | tf_op jit(solution)/shard_map/all_gather | solution.py:128
  73.4 3.7 collective-permute-done.1
  79.5 1.9 collective-permute-start.3
  81.4 3.9 collective-permute-start.2
  85.6 2.3 collective-permute-done.3
  90.4 4.2 collective-permute-start.5
  94.6 1.9 collective-permute-start.4
  97.3 3.2 collective-permute-done.4
  102.3 3.2 collective-permute-start.6
  107.0 5.1 collective-permute-done.7
  114.2 5.6 collective-permute-start.9
  122.3 4.4 collective-permute-done.8
  128.6 3.2 collective-permute-start.10
  133.3 2.3 collective-permute-done.11
  137.7 3.9 collective-permute-start.13
  141.6 1.9 collective-permute-start.12
  144.2 3.2 collective-permute-done.12
  149.2 3.0 collective-permute-start.14
  153.7 2.5 collective-permute-done.15
  158.3 3.1 collective-permute-start.17
  161.5 2.7 collective-permute-start.16
  164.9 2.4 collective-permute-done.16
  169.1 3.0 collective-permute-start.18
  173.6 2.5 collective-permute-done.19
  178.2 3.1 collective-permute-start.21
  181.3 2.7 collective-permute-start.20
  184.8 2.4 collective-permute-done.20
  189.0 3.0 collective-permute-start.22
  193.5 2.7 collective-permute-done.23
  198.3 3.1 collective-permute-start.25
  201.4 2.7 collective-permute-start.24
  204.8 2.4 collective-permute-done.24
  209.0 3.0 collective-permute-start.26
  213.5 3.8 collective-permute-done.27
  219.3 3.1 collective-permute-start.29
  222.5 2.7 collective-permute-start.28
  225.9 2.4 collective-permute-done.28
  230.1 3.0 collective-permute-start.30
  234.6 3.8 collective-permute-done.31
  240.4 3.1 collective-permute-start.33
  243.6 2.7 collective-permute-start.32
  247.1 2.2 collective-permute-done.32
  251.4 3.0 collective-permute-start.34
  257.0 2.6 collective-permute-done.35
  262.1 84.7 %all-reduce.20.cloned.1.call-done = f32[8,12288]{1,0:T(8,128)} async-done(((f32[8,12288]{1,0:T(8,128)}), f32[8,12288]{1,0:T(8,128)}) %all-reduce.20.cloned.1.call-update) | async-done | bytes 393232
  348.5 246.2 %psum.7 = f32[1,12288]{1,0:T(1,128)S(1)} all-reduce(f32[1,12288]{1,0:T(1,128)S(1)} %constant_dynamic-slice_fusion), channel_id=1, replica_groups=mesh['segment'=8,'gy'=64] {'gy'}, use_global_device_ids=true, to_apply=%region_2.3 | all-reduce | flops 12288 | bytes 98304 | tf_op jit(solution)/shard_map/psum | solution.py:157
  (326 shorter events, 64.5 us)
Async XLA Ops:
  7.2 10.0 %copy-start.3 = (s32[1,12]{1,0:T(1,128)S(1)}, s32[1,12]{1,0:T(1,128)}, u32[]{:S(2)}) copy-start(s32[1,12]{1,0:T(1,128)} %param.9) | copy-start | bytes 148
  7.2 63.5 %all-to-all-start = ((bf16[1,8,2,32,256]{4,3,2,0,1:T(8,128)(2,1)}), bf16[1,8,2,32,256]{4,3,2,0,1:T(8,128)(2,1)S(1)}, u32[]{:S(2)}, u32[]{:S(2)}) async-start(bf16[1,8,2,32,256]{4,3,2,0,1:T(8,128)(2,1)} %bitcast.2011), calls=%async_computation | async-start | bytes 524288 | tf_op jit(solution)/shard_map/all_to_all | solution.py:127
  17.2 1.5 copy-start.2
  17.2 329.7 %all-reduce.20.cloned.1.call-start = ((), (), s32[]{:S(2)}) async-start(), calls=%async_computation.1 | async-start | bytes 786432
  18.6 26.2 %copy-start.1 = (bf16[1,3,3,32,32]{4,3,2,1,0:T(8,128)(2,1)S(1)}, bf16[1,3,3,32,32]{4,3,2,1,0:T(8,128)(2,1)}, u32[]{:S(2)}) copy-start(bf16[1,3,3,32,32]{4,3,2,1,0:T(8,128)(2,1)} %param.7) | copy-start | bytes 55300
  70.7 2.7 collective-permute-start
  72.0 5.0 collective-permute-start.1
  79.5 8.4 %collective-permute-start.3 = (bf16[8,1,2,32,256]{4,3,2,0,1:T(8,128)(2,1)S(1)}, bf16[8,1,2,32,256]{4,3,2,0,1:T(8,128)(2,1)S(1)}, u32[]{:S(2)}, u32[]{:S(2)}) collective-permute-start(bf16[8,1,2,32,256]{4,3,2,0,1:T(8,128)(2,1)S(1)} %bitcast.1994), channel_id=1, source_target_pairs={{64,0},{128,64},{192,128},{256,192},{320,256},{384,320},{448,384},... | collective-permute-start | bytes 786440 | tf_op jit(solution)/shard_map/ppermute | solution.py:18
  81.4 8.4 %collective-permute-start.2 = (bf16[8,1,2,32,256]{4,3,2,0,1:T(8,128)(2,1)S(1)}, bf16[8,1,2,32,256]{4,3,2,0,1:T(8,128)(2,1)S(1)}, u32[]{:S(2)}, u32[]{:S(2)}) collective-permute-start(bf16[8,1,2,32,256]{4,3,2,0,1:T(8,128)(2,1)S(1)} %bitcast.1995), channel_id=1, source_target_pairs={{0,64},{64,128},{128,192},{192,256},{256,320},{320,384},{384,448},... | collective-permute-start | bytes 786440 | tf_op jit(solution)/shard_map/ppermute | solution.py:15
  88.1 2.1 copy-start
  90.4 6.6 %collective-permute-start.5 = (bf16[1,2,32,256]{3,2,1,0:T(8,128)(2,1)S(1)}, bf16[1,2,32,256]{3,2,1,0:T(8,128)(2,1)S(1)}, u32[]{:S(2)}, u32[]{:S(2)}) collective-permute-start(bf16[1,2,32,256]{3,2,1,0:T(8,128)(2,1)S(1)} %fusion.86), channel_id=1, source_target_pairs={{0,64},{64,128},{128,192},{192,256},{256,320},{320,384},{384,448},... | collective-permute-start | bytes 98312 | tf_op jit(solution)/shard_map/ppermute | solution.py:15
  94.6 5.8 collective-permute-start.4
  102.3 4.7 collective-permute-start.6
  105.5 6.6 %collective-permute-start.7 = (bf16[1,1,32,256]{3,2,1,0:T(8,128)(2,1)S(1)}, bf16[1,1,32,256]{3,2,1,0:T(8,128)(2,1)S(1)}, u32[]{:S(2)}, u32[]{:S(2)}) collective-permute-start(bf16[1,1,32,256]{3,2,1,0:T(8,128)(2,1)S(1)} %get-tuple-element.36), channel_id=1, source_target_pairs={{1,0},{2,1},{3,2},{4,3},{5,4},{6,5},{7,6},{8,7},{9,8},{10,9},{11,1... | collective-permute-start | bytes 49160 | tf_op jit(solution)/shard_map/ppermute | solution.py:18
  114.2 8.0 %collective-permute-start.9 = (bf16[1,2,32,256]{3,2,1,0:T(8,128)(2,1)S(1)}, bf16[1,2,32,256]{3,2,1,0:T(8,128)(2,1)S(1)}, u32[]{:S(2)}, u32[]{:S(2)}) collective-permute-start(bf16[1,2,32,256]{3,2,1,0:T(8,128)(2,1)S(1)} %get-tuple-element.37), channel_id=1, source_target_pairs={{0,64},{64,128},{128,192},{192,256},{256,320},{320,384},{384,448},... | collective-permute-start | bytes 98312 | tf_op jit(solution)/shard_map/ppermute | solution.py:15
  119.7 7.0 %collective-permute-start.8 = (bf16[1,2,32,256]{3,2,1,0:T(8,128)(2,1)S(1)}, bf16[1,2,32,256]{3,2,1,0:T(8,128)(2,1)S(1)}, u32[]{:S(2)}, u32[]{:S(2)}) collective-permute-start(bf16[1,2,32,256]{3,2,1,0:T(8,128)(2,1)S(1)} %get-tuple-element.37), channel_id=1, source_target_pairs={{64,0},{128,64},{192,128},{256,192},{320,256},{384,320},{448,384},... | collective-permute-start | bytes 98312 | tf_op jit(solution)/shard_map/ppermute | solution.py:18
  128.6 4.7 collective-permute-start.10
  131.8 3.8 collective-permute-start.11
  137.7 6.4 %collective-permute-start.13 = (bf16[1,2,32,256]{3,2,1,0:T(8,128)(2,1)S(1)}, bf16[1,2,32,256]{3,2,1,0:T(8,128)(2,1)S(1)}, u32[]{:S(2)}, u32[]{:S(2)}) collective-permute-start(bf16[1,2,32,256]{3,2,1,0:T(8,128)(2,1)S(1)} %get-tuple-element.39), channel_id=1, source_target_pairs={{0,64},{64,128},{128,192},{192,256},{256,320},{320,384},{384,448},... | collective-permute-start | bytes 98312 | tf_op jit(solution)/shard_map/ppermute | solution.py:15
  141.6 5.8 collective-permute-start.12
  149.2 4.4 collective-permute-start.14
  152.2 4.0 collective-permute-start.15
  158.3 6.3 %collective-permute-start.17 = (bf16[1,2,32,256]{3,2,1,0:T(8,128)(2,1)S(1)}, bf16[1,2,32,256]{3,2,1,0:T(8,128)(2,1)S(1)}, u32[]{:S(2)}, u32[]{:S(2)}) collective-permute-start(bf16[1,2,32,256]{3,2,1,0:T(8,128)(2,1)S(1)} %get-tuple-element.41), channel_id=1, source_target_pairs={{0,64},{64,128},{128,192},{192,256},{256,320},{320,384},{384,448},... | collective-permute-start | bytes 98312 | tf_op jit(solution)/shard_map/ppermute | solution.py:15
  161.5 5.8 collective-permute-start.16
  169.1 4.4 collective-permute-start.18
  172.1 4.0 collective-permute-start.19
  178.2 6.3 %collective-permute-start.21 = (bf16[1,2,32,256]{3,2,1,0:T(8,128)(2,1)S(1)}, bf16[1,2,32,256]{3,2,1,0:T(8,128)(2,1)S(1)}, u32[]{:S(2)}, u32[]{:S(2)}) collective-permute-start(bf16[1,2,32,256]{3,2,1,0:T(8,128)(2,1)S(1)} %get-tuple-element.43), channel_id=1, source_target_pairs={{0,64},{64,128},{128,192},{192,256},{256,320},{320,384},{384,448},... | collective-permute-start | bytes 98312 | tf_op jit(solution)/shard_map/ppermute | solution.py:15
  181.3 5.8 collective-permute-start.20
  189.0 4.4 collective-permute-start.22
  192.0 4.2 collective-permute-start.23
  198.3 6.3 %collective-permute-start.25 = (bf16[1,2,32,256]{3,2,1,0:T(8,128)(2,1)S(1)}, bf16[1,2,32,256]{3,2,1,0:T(8,128)(2,1)S(1)}, u32[]{:S(2)}, u32[]{:S(2)}) collective-permute-start(bf16[1,2,32,256]{3,2,1,0:T(8,128)(2,1)S(1)} %get-tuple-element.45), channel_id=1, source_target_pairs={{0,64},{64,128},{128,192},{192,256},{256,320},{320,384},{384,448},... | collective-permute-start | bytes 98312 | tf_op jit(solution)/shard_map/ppermute | solution.py:15
  201.4 5.8 collective-permute-start.24
  209.0 4.4 collective-permute-start.26
  212.0 5.2 collective-permute-start.27
  219.3 6.3 %collective-permute-start.29 = (bf16[1,2,32,256]{3,2,1,0:T(8,128)(2,1)S(1)}, bf16[1,2,32,256]{3,2,1,0:T(8,128)(2,1)S(1)}, u32[]{:S(2)}, u32[]{:S(2)}) collective-permute-start(bf16[1,2,32,256]{3,2,1,0:T(8,128)(2,1)S(1)} %get-tuple-element.47), channel_id=1, source_target_pairs={{0,64},{64,128},{128,192},{192,256},{256,320},{320,384},{384,448},... | collective-permute-start | bytes 98312 | tf_op jit(solution)/shard_map/ppermute | solution.py:15
  222.5 5.8 collective-permute-start.28
  230.1 4.4 collective-permute-start.30
  233.1 5.2 collective-permute-start.31
  240.4 6.5 %collective-permute-start.33 = (bf16[1,2,32,256]{3,2,1,0:T(8,128)(2,1)S(1)}, bf16[1,2,32,256]{3,2,1,0:T(8,128)(2,1)S(1)}, u32[]{:S(2)}, u32[]{:S(2)}) collective-permute-start(bf16[1,2,32,256]{3,2,1,0:T(8,128)(2,1)S(1)} %get-tuple-element.49), channel_id=1, source_target_pairs={{0,64},{64,128},{128,192},{192,256},{256,320},{320,384},{384,448},... | collective-permute-start | bytes 98312 | tf_op jit(solution)/shard_map/ppermute | solution.py:15
  243.6 5.8 collective-permute-start.32
  251.4 5.6 collective-permute-start.34
  254.4 5.2 collective-permute-start.35
Sparse Core Ops, SparseCore 0:
  257.1 89.6 all-reduce.19
where the time goes:
time: 604 us; the launch traced here: 603 us
  blocking collectives  298 us (49%)
  waiting for transfers between devices  140 us (23%)
  starting transfers between devices  101 us (17%)
  matrix products  38.6 us (6%)
  between operations  15.3 us (3%)
  local copies, waits for them, and re-layouts  7.11 us (1%)
    psum x1, blocking collectives, local(): flat = lax.psum(flat, 'gy')  246 us
    unnamed x2, waiting for transfers between devices  84.7 us
    ppermute x18, starting transfers between devices, padded_2(): lax.ppermute(lax.slice_in_dim(block, block.shape[dim] - width, None, axis...  58.6 us
    ppermute x18, waiting for transfers between devices, padded_2(): lax.ppermute(lax.slice_in_dim(block, 0, width, axis=dim), axis, backward)  53.8 us
    ppermute x18, starting transfers between devices, padded_2(): lax.ppermute(lax.slice_in_dim(block, 0, width, axis=dim), axis, backward)  32.9 us
    all_gather x1, blocking collectives, local(): depth_w = lax.all_gather(w_depth, 'segment', axis=0, tiled=True)  26.2 us
    all_gather x1, blocking collectives, local(): plane_w = lax.all_gather(w_plane, 'segment', axis=0, tiled=True)  25.8 us
    dot_general x72, matrix products, plane_back(): jnp.einsum('oc,...yox->...ycx', kernel[i, j], padded[..., 2 - i:2 - i + h...  15 us
  transfers between devices with their start and end apart: 38, of which 20 were waited for; matrix products, arithmetic and copies ran while one was open for 2% of the time, Pallas kernels for 0%

commit v1 on v0

--- a/solution.py
+++ b/solution.py
@@ -125,7 +125,16 @@
     scale = 1.0 / math.sqrt(sections * height * lax.axis_size("gy") * width)
     segment = lax.axis_index("segment")
     mine = lax.all_to_all(acts, "segment", 1, 0, tiled=True)
-    plane_w = lax.all_gather(w_plane, "segment", axis=0, tiled=True)
+    ways = lax.axis_size("segment")
+    up = [(d, (d + 1) % ways) for d in range(ways)]
+    down = [(d, (d - 1) % ways) for d in range(ways)]
+    earlier, later = ([w_plane], [w_plane])
+    for _ in range(ways // 2):
+        earlier.append(lax.ppermute(earlier[-1], "segment", up))
+    for _ in range((ways - 1) // 2):
+        later.append(lax.ppermute(later[-1], "segment", down))
+    line = jnp.concatenate([*earlier[::-1], *later[1:]], axis=0)
+    plane_w = jnp.roll(line, (lax.axis_index("segment") - ways // 2) * w_plane.shape[0], axis=0)
     depth_w = lax.all_gather(w_depth, "segment", axis=0, tiled=True)
     ids = (segment * zs + jnp.arange(zs, dtype=jnp.int32))[:, None] * (width // TILE) + jnp.arange(
         width // TILE, dtype=jnp.int32

time: 604 us -> 611 us (1.012)
  blocking collectives: 298 us -> 274 us
  starting transfers between devices: 101 us -> 123 us
  waiting for transfers between devices: 140 us -> 148 us
    all_gather x1 -> x0, blocking collectives: 25.8 us -> none  [local(): plane_w = lax.all_gather(w_plane, 'segment', axis=0, tiled=True)]
    ppermute x0 -> x7, starting transfers between devices: none -> 23.3 us  [the longest x4 13.6 us: local(): earlier.append(lax.ppermute(earlier[-1], 'segment', up))]
    ppermute x0 -> x7, waiting for transfers between devices: none -> 7.03 us  [the longest x3 4.17 us: local(): later.append(lax.ppermute(later[-1], 'segment', down))]
  transfers between devices with their start and end apart: 38 -> 45, of which waited for: 20 -> 22; matrix products, arithmetic and copies ran while one was open for 2% -> 2% of each run, Pallas kernels for 0% -> 0%
where the time goes in v1:
time: 611 us; the launch traced here: 609 us
  blocking collectives  274 us (45%)
  waiting for transfers between devices  148 us (24%)
  starting transfers between devices  123 us (20%)
  matrix products  38.6 us (6%)
  between operations  15.4 us (3%)
  local copies, waits for them, and re-layouts  7.36 us (1%)
    psum x1, blocking collectives, local(): flat = lax.psum(flat, 'gy')  246 us
    unnamed x2, waiting for transfers between devices  84.7 us
    ppermute x18, starting transfers between devices, padded_2(): lax.ppermute(lax.slice_in_dim(block, block.shape[dim] - width, None, axis...  57.6 us
    ppermute x18, waiting for transfers between devices, padded_2(): lax.ppermute(lax.slice_in_dim(block, 0, width, axis=dim), axis, backward)  54.1 us
    ppermute x18, starting transfers between devices, padded_2(): lax.ppermute(lax.slice_in_dim(block, 0, width, axis=dim), axis, backward)  33.9 us
    all_gather x1, blocking collectives, local(): depth_w = lax.all_gather(w_depth, 'segment', axis=0, tiled=True)  27.8 us
    dot_general x72, matrix products, plane_back(): jnp.einsum('oc,...yox->...ycx', kernel[i, j], padded[..., 2 - i:2 - i + h...  14.9 us
    ppermute x4, starting transfers between devices, local(): earlier.append(lax.ppermute(earlier[-1], 'segment', up))  13.6 us
  transfers between devices with their start and end apart: 45, of which 22 were waited for; matrix products, arithmetic and copies ran while one was open for 2% of the time, Pallas kernels for 0%

profile of v1, /device:TPU:64, one launch (start us, length us, event | category | flops | bytes accessed | tf_op | source)
XLA Modules:
  0.0 609.4 jit_solution(10289231182906690298)
XLA Ops:
  7.2 4.4 collective-permute-start.2
  11.6 4.6 collective-permute-start.6
  16.2 8.1 %all-to-all-start = ((bf16[1,8,2,32,256]{4,3,2,0,1:T(8,128)(2,1)}), bf16[1,8,2,32,256]{4,3,2,0,1:T(8,128)(2,1)S(1)}, u32[]{:S(2)}, u32[]{:S(2)}) async-start(bf16[1,8,2,32,256]{4,3,2,0,1:T(8,128)(2,1)} %bitcast.2020), calls=%async_computation | async-start | bytes 524288 | tf_op jit(solution)/shard_map/all_to_all | solution.py:127
  24.3 3.4 collective-permute-start.3
  28.6 2.9 collective-permute-done.3
  31.4 3.2 collective-permute-start.4
  35.9 3.1 collective-permute-start.7
  39.1 2.7 collective-permute-start.5
  41.8 27.8 %all_gather.3 = bf16[8,3,32,32]{3,2,0,1:T(8,128)(2,1)S(1)} all-gather(bf16[1,3,32,32]{3,2,0,1:T(8,128)(2,1)} %bitcast.2021), channel_id=1, replica_groups=mesh['segment'=8,'gy'=64] {'segment'}, dimensions={0}, use_global_device_ids=true | all-gather | bytes 55296 | tf_op jit(solution)/shard_map/all_gather | solution.py:138
  71.6 4.2 collective-permute-done.8
  78.9 3.5 collective-permute-done.1
  87.1 3.5 collective-permute-start.9
  93.4 2.4 collective-permute-done.9
  96.4 3.5 collective-permute-start.12
  102.9 3.8 collective-permute-done.11
  108.6 3.2 collective-permute-start.13
  113.3 5.0 collective-permute-done.14
  120.4 5.6 collective-permute-start.16
  128.6 4.4 collective-permute-done.15
  134.9 3.2 collective-permute-start.17
  144.0 3.9 collective-permute-start.20
  150.5 3.2 collective-permute-done.19
  155.5 3.0 collective-permute-start.21
  160.0 2.5 collective-permute-done.22
  164.6 3.1 collective-permute-start.24
  167.8 2.7 collective-permute-start.23
  175.4 3.0 collective-permute-start.25
  179.9 2.5 collective-permute-done.26
  184.5 3.1 collective-permute-start.28
  187.6 2.7 collective-permute-start.27
  191.0 2.4 collective-permute-done.27
  195.3 3.0 collective-permute-start.29
  199.7 2.7 collective-permute-done.30
  204.5 3.1 collective-permute-start.32
  207.7 2.7 collective-permute-start.31
  215.3 3.0 collective-permute-start.33
  219.8 3.8 collective-permute-done.34
  225.6 3.1 collective-permute-start.36
  228.7 2.7 collective-permute-start.35
  232.1 2.4 collective-permute-done.35
  236.4 3.0 collective-permute-start.37
  241.0 3.6 collective-permute-done.38
  246.7 3.1 collective-permute-start.40
  249.8 2.7 collective-permute-start.39
  257.6 3.0 collective-permute-start.41
  263.2 2.6 collective-permute-done.42
  268.4 84.7 %all-reduce.20.cloned.1.call-done = f32[8,12288]{1,0:T(8,128)} async-done(((f32[8,12288]{1,0:T(8,128)}), f32[8,12288]{1,0:T(8,128)}) %all-reduce.20.cloned.1.call-update) | async-done | bytes 393232
  354.8 246.2 %psum.7 = f32[1,12288]{1,0:T(1,128)S(1)} all-reduce(f32[1,12288]{1,0:T(1,128)S(1)} %constant_dynamic-slice_fusion), channel_id=1, replica_groups=mesh['segment'=8,'gy'=64] {'gy'}, use_global_device_ids=true, to_apply=%region_2.3 | all-reduce | flops 12288 | bytes 98304 | tf_op jit(solution)/shard_map/psum | solution.py:166
  (351 shorter events, 84.0 us)
Async XLA Ops:
  7.2 64.4 %copy-start = (bf16[1,3,3,32,32]{4,3,2,1,0:T(8,128)(2,1)S(1)}, bf16[1,3,3,32,32]{4,3,2,1,0:T(8,128)(2,1)}, u32[]{:S(2)}) copy-start(bf16[1,3,3,32,32]{4,3,2,1,0:T(8,128)(2,1)} %param.7) | copy-start | bytes 55300
  7.2 17.2 %collective-permute-start.2 = (bf16[1,3,3,32,32]{4,3,0,2,1:T(8,128)(2,1)}, bf16[1,3,3,32,32]{4,3,0,2,1:T(8,128)(2,1)S(1)}, u32[]{:S(2)}, u32[]{:S(2)}) collective-permute-start(bf16[1,3,3,32,32]{4,3,0,2,1:T(8,128)(2,1)} %bitcast.2018), channel_id=1, source_target_pairs={{0,64},{64,128},{128,192},{192,256},{256,320},{320,384},{384,448},... | collective-permute-start | bytes 55304 | tf_op jit(solution)/shard_map/ppermute | solution.py:133
  11.6 24.3 %collective-permute-start.6 = (bf16[1,3,3,32,32]{4,3,0,2,1:T(8,128)(2,1)}, bf16[1,3,3,32,32]{4,3,0,2,1:T(8,128)(2,1)S(1)}, u32[]{:S(2)}, u32[]{:S(2)}) collective-permute-start(bf16[1,3,3,32,32]{4,3,0,2,1:T(8,128)(2,1)} %bitcast.2019), channel_id=1, source_target_pairs={{0,448},{64,0},{128,64},{192,128},{256,192},{320,256},{384,320},{4... | collective-permute-start | bytes 55304 | tf_op jit(solution)/shard_map/ppermute | solution.py:135
  16.2 59.9 %all-to-all-start = ((bf16[1,8,2,32,256]{4,3,2,0,1:T(8,128)(2,1)}), bf16[1,8,2,32,256]{4,3,2,0,1:T(8,128)(2,1)S(1)}, u32[]{:S(2)}, u32[]{:S(2)}) async-start(bf16[1,8,2,32,256]{4,3,2,0,1:T(8,128)(2,1)} %bitcast.2020), calls=%async_computation | async-start | bytes 524288 | tf_op jit(solution)/shard_map/all_to_all | solution.py:127
  24.3 328.8 %all-reduce.20.cloned.1.call-start = ((), (), s32[]{:S(2)}) async-start(), calls=%async_computation.1 | async-start | bytes 786432
  24.3 7.1 %collective-permute-start.3 = (bf16[1,3,3,32,32]{4,3,0,2,1:T(8,128)(2,1)S(1)}, bf16[1,3,3,32,32]{4,3,0,2,1:T(8,128)(2,1)S(1)}, u32[]{:S(2)}, u32[]{:S(2)}) collective-permute-start(bf16[1,3,3,32,32]{4,3,0,2,1:T(8,128)(2,1)S(1)} %collective-permute-done.2), channel_id=1, source_target_pairs={{0,64},{64,128},{128,192},{192,256},{256,320},{320,384},{384,448},... | collective-permute-start | bytes 55304 | tf_op jit(solution)/shard_map/ppermute | solution.py:133
  31.4 7.6 %collective-permute-start.4 = (bf16[1,3,3,32,32]{4,3,0,2,1:T(8,128)(2,1)S(1)}, bf16[1,3,3,32,32]{4,3,0,2,1:T(8,128)(2,1)S(1)}, u32[]{:S(2)}, u32[]{:S(2)}) collective-permute-start(bf16[1,3,3,32,32]{4,3,0,2,1:T(8,128)(2,1)S(1)} %collective-permute-done.3), channel_id=1, source_target_pairs={{0,64},{64,128},{128,192},{192,256},{256,320},{320,384},{384,448},... | collective-permute-start | bytes 55304 | tf_op jit(solution)/shard_map/ppermute | solution.py:133
  35.9 33.6 %collective-permute-start.7 = (bf16[1,3,3,32,32]{4,3,0,2,1:T(8,128)(2,1)S(1)}, bf16[1,3,3,32,32]{4,3,0,2,1:T(8,128)(2,1)S(1)}, u32[]{:S(2)}, u32[]{:S(2)}) collective-permute-start(bf16[1,3,3,32,32]{4,3,0,2,1:T(8,128)(2,1)S(1)} %collective-permute-done.6), channel_id=1, source_target_pairs={{0,448},{64,0},{128,64},{192,128},{256,192},{320,256},{384,320},{4... | collective-permute-start | bytes 55304 | tf_op jit(solution)/shard_map/ppermute | solution.py:135
  39.1 32.4 %collective-permute-start.5 = (bf16[1,3,3,32,32]{4,3,0,2,1:T(8,128)(2,1)S(1)}, bf16[1,3,3,32,32]{4,3,0,2,1:T(8,128)(2,1)S(1)}, u32[]{:S(2)}, u32[]{:S(2)}) collective-permute-start(bf16[1,3,3,32,32]{4,3,0,2,1:T(8,128)(2,1)S(1)} %collective-permute-done.4), channel_id=1, source_target_pairs={{0,64},{64,128},{128,192},{192,256},{256,320},{320,384},{384,448},... | collective-permute-start | bytes 55304 | tf_op jit(solution)/shard_map/ppermute | solution.py:133
  69.6 6.2 %collective-permute-start.8 = (bf16[1,3,3,32,32]{4,3,0,2,1:T(8,128)(2,1)S(1)}, bf16[1,3,3,32,32]{4,3,0,2,1:T(8,128)(2,1)S(1)}, u32[]{:S(2)}, u32[]{:S(2)}) collective-permute-start(bf16[1,3,3,32,32]{4,3,0,2,1:T(8,128)(2,1)S(1)} %collective-permute-done.7), channel_id=1, source_target_pairs={{0,448},{64,0},{128,64},{192,128},{256,192},{320,256},{384,320},{4... | collective-permute-start | bytes 55304 | tf_op jit(solution)/shard_map/ppermute | solution.py:135
  76.1 2.8 collective-permute-start
  77.4 5.0 collective-permute-start.1
  84.7 8.4 %collective-permute-start.10 = (bf16[8,1,2,32,256]{4,3,2,0,1:T(8,128)(2,1)S(1)}, bf16[8,1,2,32,256]{4,3,2,0,1:T(8,128)(2,1)S(1)}, u32[]{:S(2)}, u32[]{:S(2)}) collective-permute-start(bf16[8,1,2,32,256]{4,3,2,0,1:T(8,128)(2,1)S(1)} %bitcast.2001), channel_id=1, source_target_pairs={{64,0},{128,64},{192,128},{256,192},{320,256},{384,320},{448,384},... | collective-permute-start | bytes 786440 | tf_op jit(solution)/shard_map/ppermute | solution.py:18
  87.1 8.7 %collective-permute-start.9 = (bf16[8,1,2,32,256]{4,3,2,0,1:T(8,128)(2,1)S(1)}, bf16[8,1,2,32,256]{4,3,2,0,1:T(8,128)(2,1)S(1)}, u32[]{:S(2)}, u32[]{:S(2)}) collective-permute-start(bf16[8,1,2,32,256]{4,3,2,0,1:T(8,128)(2,1)S(1)} %bitcast.2002), channel_id=1, source_target_pairs={{0,64},{64,128},{128,192},{192,256},{256,320},{320,384},{384,448},... | collective-permute-start | bytes 786440 | tf_op jit(solution)/shard_map/ppermute | solution.py:15
  93.4 2.8 copy-start.1
  96.4 6.3 %collective-permute-start.12 = (bf16[1,2,32,256]{3,2,1,0:T(8,128)(2,1)S(1)}, bf16[1,2,32,256]{3,2,1,0:T(8,128)(2,1)S(1)}, u32[]{:S(2)}, u32[]{:S(2)}) collective-permute-start(bf16[1,2,32,256]{3,2,1,0:T(8,128)(2,1)S(1)} %fusion.97), channel_id=1, source_target_pairs={{0,64},{64,128},{128,192},{192,256},{256,320},{320,384},{384,448},... | collective-permute-start | bytes 98312 | tf_op jit(solution)/shard_map/ppermute | solution.py:15
  99.9 6.8 %collective-permute-start.11 = (bf16[1,2,32,256]{3,2,1,0:T(8,128)(2,1)S(1)}, bf16[1,2,32,256]{3,2,1,0:T(8,128)(2,1)S(1)}, u32[]{:S(2)}, u32[]{:S(2)}) collective-permute-start(bf16[1,2,32,256]{3,2,1,0:T(8,128)(2,1)S(1)} %fusion.97), channel_id=1, source_target_pairs={{64,0},{128,64},{192,128},{256,192},{320,256},{384,320},{448,384},... | collective-permute-start | bytes 98312 | tf_op jit(solution)/shard_map/ppermute | solution.py:18
  108.6 4.7 collective-permute-start.13
  111.8 6.5 %collective-permute-start.14 = (bf16[1,1,32,256]{3,2,1,0:T(8,128)(2,1)S(1)}, bf16[1,1,32,256]{3,2,1,0:T(8,128)(2,1)S(1)}, u32[]{:S(2)}, u32[]{:S(2)}) collective-permute-start(bf16[1,1,32,256]{3,2,1,0:T(8,128)(2,1)S(1)} %get-tuple-element.36), channel_id=1, source_target_pairs={{1,0},{2,1},{3,2},{4,3},{5,4},{6,5},{7,6},{8,7},{9,8},{10,9},{11,1... | collective-permute-start | bytes 49160 | tf_op jit(solution)/shard_map/ppermute | solution.py:18
  120.4 8.0 %collective-permute-start.16 = (bf16[1,2,32,256]{3,2,1,0:T(8,128)(2,1)S(1)}, bf16[1,2,32,256]{3,2,1,0:T(8,128)(2,1)S(1)}, u32[]{:S(2)}, u32[]{:S(2)}) collective-permute-start(bf16[1,2,32,256]{3,2,1,0:T(8,128)(2,1)S(1)} %get-tuple-element.37), channel_id=1, source_target_pairs={{0,64},{64,128},{128,192},{192,256},{256,320},{320,384},{384,448},... | collective-permute-start | bytes 98312 | tf_op jit(solution)/shard_map/ppermute | solution.py:15
  126.0 7.0 %collective-permute-start.15 = (bf16[1,2,32,256]{3,2,1,0:T(8,128)(2,1)S(1)}, bf16[1,2,32,256]{3,2,1,0:T(8,128)(2,1)S(1)}, u32[]{:S(2)}, u32[]{:S(2)}) collective-permute-start(bf16[1,2,32,256]{3,2,1,0:T(8,128)(2,1)S(1)} %get-tuple-element.37), channel_id=1, source_target_pairs={{64,0},{128,64},{192,128},{256,192},{320,256},{384,320},{448,384},... | collective-permute-start | bytes 98312 | tf_op jit(solution)/shard_map/ppermute | solution.py:18
  134.9 4.7 collective-permute-start.17
  138.1 3.8 collective-permute-start.18
  144.0 6.3 %collective-permute-start.20 = (bf16[1,2,32,256]{3,2,1,0:T(8,128)(2,1)S(1)}, bf16[1,2,32,256]{3,2,1,0:T(8,128)(2,1)S(1)}, u32[]{:S(2)}, u32[]{:S(2)}) collective-permute-start(bf16[1,2,32,256]{3,2,1,0:T(8,128)(2,1)S(1)} %get-tuple-element.39), channel_id=1, source_target_pairs={{0,64},{64,128},{128,192},{192,256},{256,320},{320,384},{384,448},... | collective-permute-start | bytes 98312 | tf_op jit(solution)/shard_map/ppermute | solution.py:15
  147.9 5.8 collective-permute-start.19
  155.5 4.4 collective-permute-start.21
  158.5 4.0 collective-permute-start.22
  164.6 6.3 %collective-permute-start.24 = (bf16[1,2,32,256]{3,2,1,0:T(8,128)(2,1)S(1)}, bf16[1,2,32,256]{3,2,1,0:T(8,128)(2,1)S(1)}, u32[]{:S(2)}, u32[]{:S(2)}) collective-permute-start(bf16[1,2,32,256]{3,2,1,0:T(8,128)(2,1)S(1)} %get-tuple-element.41), channel_id=1, source_target_pairs={{0,64},{64,128},{128,192},{192,256},{256,320},{320,384},{384,448},... | collective-permute-start | bytes 98312 | tf_op jit(solution)/shard_map/ppermute | solution.py:15
  167.8 5.8 collective-permute-start.23
  175.4 4.4 collective-permute-start.25
  178.4 4.0 collective-permute-start.26
  184.5 6.3 %collective-permute-start.28 = (bf16[1,2,32,256]{3,2,1,0:T(8,128)(2,1)S(1)}, bf16[1,2,32,256]{3,2,1,0:T(8,128)(2,1)S(1)}, u32[]{:S(2)}, u32[]{:S(2)}) collective-permute-start(bf16[1,2,32,256]{3,2,1,0:T(8,128)(2,1)S(1)} %get-tuple-element.43), channel_id=1, source_target_pairs={{0,64},{64,128},{128,192},{192,256},{256,320},{320,384},{384,448},... | collective-permute-start | bytes 98312 | tf_op jit(solution)/shard_map/ppermute | solution.py:15
  187.6 5.8 collective-permute-start.27
  195.3 4.4 collective-permute-start.29
  198.2 4.2 collective-permute-start.30
  204.5 6.3 %collective-permute-start.32 = (bf16[1,2,32,256]{3,2,1,0:T(8,128)(2,1)S(1)}, bf16[1,2,32,256]{3,2,1,0:T(8,128)(2,1)S(1)}, u32[]{:S(2)}, u32[]{:S(2)}) collective-permute-start(bf16[1,2,32,256]{3,2,1,0:T(8,128)(2,1)S(1)} %get-tuple-element.45), channel_id=1, source_target_pairs={{0,64},{64,128},{128,192},{192,256},{256,320},{320,384},{384,448},... | collective-permute-start | bytes 98312 | tf_op jit(solution)/shard_map/ppermute | solution.py:15
  207.7 5.8 collective-permute-start.31
  215.3 4.4 collective-permute-start.33
  218.3 5.2 collective-permute-start.34
  225.6 6.3 %collective-permute-start.36 = (bf16[1,2,32,256]{3,2,1,0:T(8,128)(2,1)S(1)}, bf16[1,2,32,256]{3,2,1,0:T(8,128)(2,1)S(1)}, u32[]{:S(2)}, u32[]{:S(2)}) collective-permute-start(bf16[1,2,32,256]{3,2,1,0:T(8,128)(2,1)S(1)} %get-tuple-element.47), channel_id=1, source_target_pairs={{0,64},{64,128},{128,192},{192,256},{256,320},{320,384},{384,448},... | collective-permute-start | bytes 98312 | tf_op jit(solution)/shard_map/ppermute | solution.py:15
  228.7 5.8 collective-permute-start.35
  236.4 4.6 collective-permute-start.37
  239.3 5.2 collective-permute-start.38
  246.7 6.5 %collective-permute-start.40 = (bf16[1,2,32,256]{3,2,1,0:T(8,128)(2,1)S(1)}, bf16[1,2,32,256]{3,2,1,0:T(8,128)(2,1)S(1)}, u32[]{:S(2)}, u32[]{:S(2)}) collective-permute-start(bf16[1,2,32,256]{3,2,1,0:T(8,128)(2,1)S(1)} %get-tuple-element.49), channel_id=1, source_target_pairs={{0,64},{64,128},{128,192},{192,256},{256,320},{320,384},{384,448},... | collective-permute-start | bytes 98312 | tf_op jit(solution)/shard_map/ppermute | solution.py:15
  249.8 5.8 collective-permute-start.39
  257.6 5.6 collective-permute-start.41
  260.6 5.2 collective-permute-start.42
Sparse Core Ops, SparseCore 0:
  263.4 89.7 all-reduce.19
